TPU v7x, 512 devices: a whole 4x8x8 slice. The times are simulated.
512 devices in a mesh: dp: 64 (over x, z, y_lo), fsdp: 8 (over y_hi, core).
Axes of the slice: x: 4, y: 8 (y_hi: 4, y_lo: 2; y = y_hi * 2 + y_lo), z: 8, core: 2. Of those that a mesh axis runs over, the one named last changes fastest.
Arguments:
- group_qkv: bfloat16 [64, 1024, 6144], P('dp', 'fsdp'), may hold values from -6 to 6
- cache_pool: bfloat16 [8192, 16, 4096], P('dp', None, 'fsdp'), may hold values from -6 to 6
- page_request: int32 [8192], P('dp'), may hold values from 0 to 64, as said below
- request_host: int32 [64], replicated, may hold values from 0 to 63, each once
- out_weight: bfloat16 [2048, 2048], P(('dp', 'fsdp')), may hold values from -0.5 to 0.5
Outputs:
- projected: bfloat16 [64, 1024, 2048], P('dp', 'fsdp')
Inputs may be any that keep to these rules, and one draw needn't show every extreme that they name: `page_request`: within the slots of one dp index, at most 2 pages belong to one request, and some request has exactly 2 pages in the slots of every dp index. A request holds 1 to 15 pages, or 64 to 128 pages. Some slot is empty.
All inputs are finite; a program needn't handle non-finite values.
Results may differ from a plain program's by a relative error of at most 0.0053.
Values may be sent and summed in bfloat16 or wider, within the bound.
No kernel may reach another device: no remote copies, remote signals or barrier semaphores. Data moves between devices by JAX's collectives and lax.ppermute only.
A program may use at most 64 MiB of HBM per device.

v0:
```python
import math
import jax
import jax.numpy as jnp
from jax import lax
from jax.sharding import Mesh, PartitionSpec as P

HD = 128
PAGE = 16
MOST = 2
PHYSICAL_SPLIT = {"dp": (("x", 4), ("z", 8), ("y_lo", 2)), "fsdp": (("y_hi", 4), ("core", 2))}
DP = tuple((name for name, _ in PHYSICAL_SPLIT["dp"]))
FSDP = tuple((name for name, _ in PHYSICAL_SPLIT["fsdp"]))


def per_device(
    group_qkv, cache_pool, page_request, request_host, out_weight, *, fsdp_count, dp_count
):
    requests = request_host.shape[0]
    slot_count = page_request.shape[0]
    tokens_here = group_qkv.shape[1]
    features = cache_pool.shape[2]
    heads_here = features // (2 * HD)
    score_scale = 1.0 / math.sqrt(HD)
    width = out_weight.shape[1]
    weight = out_weight
    for name in reversed(DP[2:] + FSDP):
        weight = lax.all_gather(weight, name, axis=0, tiled=True)
    weight, group_qkv = lax.optimization_barrier((weight, group_qkv))
    weight = lax.all_gather(weight, DP[1], axis=0, tiled=True)
    local_qkv = group_qkv.reshape(tokens_here, fsdp_count, heads_here * 3 * HD)
    gathered_qkv = lax.all_to_all(local_qkv, FSDP, split_axis=1, concat_axis=0, tiled=True)
    group_len = tokens_here * fsdp_count
    gathered_qkv = gathered_qkv.reshape(group_len, heads_here, 3, HD)
    request_ids = jnp.arange(requests, dtype=jnp.int32)
    member = (page_request[:, None] == request_ids[None, :]).astype(jnp.int32)
    slot_rank = jnp.sum(member * (jnp.cumsum(member, axis=0) - 1), axis=1)
    target_host = jnp.sum(member * request_host[None, :], axis=1)
    is_live = jnp.sum(member, axis=1)
    target_slot = jnp.where(is_live > 0, target_host * MOST + slot_rank, -1)
    chosen = target_slot[:, None] == jnp.arange(requests * MOST, dtype=jnp.int32)[None, :]
    flat_pool = cache_pool.reshape(slot_count, PAGE * features)
    packed = jnp.einsum(
        "sp,sf->pf", chosen.astype(jnp.bfloat16), flat_pool, preferred_element_type=jnp.float32
    )
    occupied = jnp.sum(chosen.astype(jnp.int32), axis=0) > 0
    packed = jnp.where(occupied[:, None], packed, jnp.nan)
    packed = packed.astype(jnp.bfloat16).reshape(requests, MOST, PAGE, features)
    weight, packed = lax.optimization_barrier((weight, packed))
    weight = lax.all_gather(weight, DP[0], axis=0, tiled=True)
    arrived = lax.all_to_all(packed, DP, split_axis=0, concat_axis=0, tiled=True)
    present = jnp.logical_not(jnp.isnan(arrived[:, :, 0, 0]))
    live_tokens = jnp.repeat(present.reshape(requests * MOST), PAGE)
    cached = arrived.reshape(requests * MOST * PAGE, heads_here, 2, HD)
    key_cache = cached[:, :, 0]
    value_cache = jnp.where(
        live_tokens[:, None, None], cached[:, :, 1], jnp.zeros((), cached.dtype)
    )
    queries = gathered_qkv[:, :, 0]
    new_keys = gathered_qkv[:, :, 1]
    new_values = gathered_qkv[:, :, 2]
    block_rows = min(512, group_len)
    block_count = group_len // block_rows
    query_blocks = queries.reshape(block_count, block_rows, heads_here, HD)

    def attend(inputs):
        query_block, first_row = inputs
        cache_scores = (
            jnp.einsum("qhd,khd->hqk", query_block, key_cache, preferred_element_type=jnp.float32)
            * score_scale
        )
        cache_scores = jnp.where(live_tokens[None, None, :], cache_scores, -jnp.inf)
        group_scores = (
            jnp.einsum("qhd,khd->hqk", query_block, new_keys, preferred_element_type=jnp.float32)
            * score_scale
        )
        causal = jnp.arange(group_len)[None, :] <= first_row + jnp.arange(block_rows)[:, None]
        group_scores = jnp.where(causal[None, :, :], group_scores, -jnp.inf)
        row_max = jnp.maximum(jnp.max(cache_scores, axis=2), jnp.max(group_scores, axis=2))
        cache_expo = jnp.exp(cache_scores - row_max[:, :, None])
        group_expo = jnp.exp(group_scores - row_max[:, :, None])
        row_total = jnp.sum(cache_expo, axis=2) + jnp.sum(group_expo, axis=2)
        mixture = jnp.einsum(
            "hqk,khd->qhd",
            cache_expo.astype(jnp.bfloat16),
            value_cache,
            preferred_element_type=jnp.float32,
        )
        mixture = mixture + jnp.einsum(
            "hqk,khd->qhd",
            group_expo.astype(jnp.bfloat16),
            new_values,
            preferred_element_type=jnp.float32,
        )
        result = mixture / jnp.transpose(row_total)[:, :, None]
        return result.astype(jnp.bfloat16).reshape(block_rows, heads_here * HD)

    starts = jnp.arange(block_count, dtype=jnp.int32) * block_rows
    attn_heads = lax.map(attend, (query_blocks, starts)).reshape(group_len, heads_here * HD)
    tokens_attn = lax.all_to_all(attn_heads, FSDP, split_axis=0, concat_axis=1, tiled=True)
    summed = jnp.dot(tokens_attn, weight, preferred_element_type=jnp.float32)
    return summed.astype(jnp.bfloat16).reshape(1, tokens_here, width)


def solution(mesh):
    split = [part for axis in mesh.axis_names for part in PHYSICAL_SPLIT[axis]]
    fine = Mesh(mesh.devices.reshape([size for _, size in split]), DP + FSDP)
    return jax.shard_map(
        lambda *args: per_device(*args, fsdp_count=mesh.shape["fsdp"], dp_count=mesh.shape["dp"]),
        mesh=fine,
        in_specs=(P(DP, FSDP, None), P(DP, None, FSDP), P(DP), P(), P(DP + FSDP, None)),
        out_specs=P(DP, FSDP, None),
        check_vma=False,
    )
```

profile of v0, /device:TPU:64, one launch (start us, length us, event | category | flops | bytes accessed | tf_op | source)
XLA Modules:
  0.0 215.4 jit_solution(14413602714746578815)
XLA Ops:
  6.5 2.0 all-gather
  8.6 16.3 %all_gather.16 = bf16[32,2048]{1,0:T(8,128)(2,1)S(1)} all-gather(bf16[8,2048]{1,0:T(8,128)(2,1)S(1)} %reshape.84), channel_id=1, replica_groups=mesh['x'=4,'z'=8,'y_lo'=2,'y_hi'=4,'core'=2] {'y_hi'}, dimensions={0}, use_global_device_ids=true | all-gather | bytes 163840 | tf_op jit(solution)/shard_map/all_gather | solution.py:27
  24.9 5.7 %all_gather.17 = bf16[64,2048]{1,0:T(8,128)(2,1)} all-gather(bf16[32,2048]{1,0:T(8,128)(2,1)S(1)} %all_gather.16), channel_id=1, replica_groups=mesh['x'=4,'z'=8,'y_lo'=2,'y_hi'=4,'core'=2] {'y_lo'}, dimensions={0}, use_global_device_ids=true | all-gather | bytes 393216 | tf_op jit(solution)/shard_map/all_gather | solution.py:27
  30.6 2.6 %copy.38 = bf16[1,128,6144]{1,2,0:T(8,128)(2,1)} copy(bf16[1,128,6144]{2,1,0:T(8,128)(2,1)} %param.7) | data formatting | bytes 3145728 | tf_op jit(solution)/shard_map/optimization_barrier | solution.py:28
  33.2 4.9 %all-to-all-start.1 = ((bf16[128,8,768]{0,2,1:T(8,128)(2,1)}), bf16[128,8,768]{0,2,1:T(8,128)(2,1)}, u32[]{:S(2)}, u32[]{:S(2)}) async-start(bf16[128,8,768]{0,2,1:T(8,128)(2,1)} %bitcast.1), calls=%async_computation.1 | async-start | bytes 3145728 | tf_op jit(solution)/shard_map/all_to_all | solution.py:31
  38.1 3.0 %copy.51 = bf16[16,8,16,512]{3,1,2,0:T(8,128)(2,1)S(1)} copy(bf16[16,8,16,512]{3,2,1,0:T(8,128)(2,1)} %bitcast.86) | data formatting | bytes 4194304
  42.5 2.2 %copy.52 = bf16[16,8,16,512]{3,2,1,0:T(8,128)(2,1)} copy(bf16[16,8,16,512]{3,1,2,0:T(8,128)(2,1)S(1)} %bitcast.82) | data formatting | bytes 4194304
  44.7 31.3 %all-gather.4.cloned.1.call-done = bf16[512,2048]{1,0:T(8,128)(2,1)} async-done(((bf16[64,2048]{1,0:T(8,128)(2,1)}), bf16[512,2048]{1,0:T(8,128)(2,1)}) %all-gather.4.cloned.1.call-update) | async-done | bytes 2097168 | tf_op jit(solution)/shard_map/all_gather | solution.py:29
  76.0 2.5 %all-to-all-done.1 = bf16[128,8,768]{0,2,1:T(8,128)(2,1)} async-done(((bf16[128,8,768]{0,2,1:T(8,128)(2,1)}), bf16[128,8,768]{0,2,1:T(8,128)(2,1)}, u32[]{:S(2)}, u32[]{:S(2)}) %all-to-all-start.1) | async-done | bytes 1572896 | tf_op jit(solution)/shard_map/all_to_all | solution.py:31
  78.6 13.5 %all-to-all-start = ((bf16[64,2,16,512]{3,2,1,0:T(8,128)(2,1)}), bf16[64,2,16,512]{3,2,1,0:T(8,128)(2,1)S(1)}, u32[]{:S(2)}, u32[]{:S(2)}) async-start(bf16[64,2,16,512]{3,2,1,0:T(8,128)(2,1)} %bitcast.83), calls=%async_computation | async-start | bytes 4194304 | tf_op jit(solution)/shard_map/all_to_all | solution.py:50
  92.8 3.6 %copy.39 = bf16[8,128,1,768]{1,0,3,2:T(8,128)(2,1)} copy(bf16[8,128,1,768]{1,3,0,2:T(8,128)(2,1)} %bitcast.3) | data formatting | bytes 3145728 | tf_op jit(solution)/shard_map/all_to_all | solution.py:31
  96.5 3.7 %reshape.80 = bf16[1024,2,3,128]{0,3,2,1:T(8,128)(2,1)} reshape(bf16[8,128,1,768]{1,0,3,2:T(8,128)(2,1)} %copy.39) | data formatting | bytes 3145728 | tf_op jit(solution)/shard_map/reshape | solution.py:33
  100.1 2.5 %slice_bitcast_fusion = (bf16[1024,2,128]{0,2,1:T(8,128)(2,1)}, bf16[1024,2,1,128]{0,3,2,1:T(8,128)(2,1)}, bf16[1024,2,1,128]{0,3,2,1:T(8,128)(2,1)S(1)}) fusion(bf16[1024,2,3,128]{0,3,2,1:T(8,128)(2,1)} %reshape.80), kind=kLoop, calls=%fused_computation.41 | loop fusion | bytes 3145728 | tf_op jit(solution)/shard_map/squeeze | solution.py:60
  104.3 37.4 %all-to-all-done = bf16[64,2,16,512]{3,2,1,0:T(8,128)(2,1)S(1)} async-done(((bf16[64,2,16,512]{3,2,1,0:T(8,128)(2,1)}), bf16[64,2,16,512]{3,2,1,0:T(8,128)(2,1)S(1)}, u32[]{:S(2)}, u32[]{:S(2)}) %all-to-all-start) | async-done | bytes 2097184 | tf_op jit(solution)/shard_map/all_to_all | solution.py:50
  141.7 2.4 %not_reduce_fusion = pred[64,2]{1,0:T(8,128)(4,1)S(1)} fusion(bf16[64,2,16,512]{3,2,1,0:T(8,128)(2,1)S(1)} %all-to-all-done), kind=kLoop, calls=%fused_computation.42 | loop fusion | flops 384 | bytes 384 | tf_op jit(solution)/shard_map/not | solution.py:51
  144.4 2.6 %reshape.81 = bf16[2048,2,2,128]{3,2,1,0:T(2,128)(2,1)S(1)} reshape(bf16[64,2,16,512]{3,2,1,0:T(8,128)(2,1)} %copy-done.1) | data formatting | bytes 4194304 | tf_op jit(solution)/shard_map/reshape | solution.py:53
  147.0 3.9 %fusion.43 = (bf16[2048,2,1,128]{3,2,1,0:T(2,128)(2,1)S(1)}, bf16[2048,2,1,128]{3,2,1,0:T(2,128)(2,1)}) fusion(bf16[2048,2,2,128]{3,2,1,0:T(2,128)(2,1)S(1)} %reshape.81), kind=kLoop, calls=%fused_computation.54 | loop fusion | bytes 4194304 | tf_op jit(solution)/shard_map/slice | solution.py:56
  154.6 27.4 %while.11 = (s32[]{:T(128)}, bf16[2,512,256]{2,1,0:T(8,128)(2,1)S(1)}, bf16[2,512,2,128]{3,1,0,2:T(8,128)(2,1)S(1)}, bf16[2048,2,128]{2,0,1:T(8,128)(2,1)S(1)}, ...) while((s32[]{:T(128)}, ...), condition=%wide.region_10.11_spmd.clone, body=%wide.region_5.10_spmd.clone.sunk | while | flops 1646131712 | bytes 69022040 | solution.py:98
  156.3 2.9 %fusion.69 = (f32[2,512]{1,0:T(2,128)S(1)}, f32[2,512,1024]{2,1,0:T(8,128)}) fusion(pred[512,1024]{1,0:T(8,128)(4,1)S(1)} %iota_compare_fusion.5, bf16[1024,2,128]{2,0,1:T(8,128)(2,1)S(1)} %get-tuple-element.236, bf16[2,512,2,128]{3,1,0,2:T(8,128)(2,1)S(1)} %get-tuple-element.233, s32[]{:T(128)} %get-tuple-element.221), kind=kOutput, calls=%fused_computation.10.clone.1 | convolution fusion | flops 271580160 | bytes 5509124 | tf_op jit(solution)/shard_map/while/body/eval_jaxpr/qhd,khd->hqk/dot_general | solution.py:73
  166.0 2.2 %fusion.74 = bf16[512,2,128]{0,2,1:T(8,128)(2,1)S(1)} fusion(f32[2,512,128]{1,2,0:T(8,128)S(1)} %fusion.71, bf16[2048,2,128]{0,2,1:T(8,128)(2,1)S(1)} %copy-done.2, f32[2,512,2048]{2,1,0:T(8,128)S(1)} %get-tuple-element.210, f32[2,512]{1,0:T(2,128)S(1)} %max.9, pred[2048]{0:T(1024)(128)(4,1)S(1)} %broadcast_in_dim.164, ...), kind=kOutput, calls=%fused_computation.19.clone.1 | convolution fusion | flops 545652736 | bytes 10233856 | tf_op jit(solution)/shard_map/while/body/eval_jaxpr/hqk,khd->qhd/dot_general | solution.py:82
  170.0 2.9 %fusion.69 = (f32[2,512]{1,0:T(2,128)S(1)}, f32[2,512,1024]{2,1,0:T(8,128)}) fusion(pred[512,1024]{1,0:T(8,128)(4,1)S(1)} %iota_compare_fusion.5, bf16[1024,2,128]{2,0,1:T(8,128)(2,1)S(1)} %get-tuple-element.236, bf16[2,512,2,128]{3,1,0,2:T(8,128)(2,1)S(1)} %get-tuple-element.233, s32[]{:T(128)} %get-tuple-element.221), kind=kOutput, calls=%fused_computation.10.clone.1 | convolution fusion | flops 271580160 | bytes 5509124 | tf_op jit(solution)/shard_map/while/body/eval_jaxpr/qhd,khd->hqk/dot_general | solution.py:73
  179.7 2.2 %fusion.74 = bf16[512,2,128]{0,2,1:T(8,128)(2,1)S(1)} fusion(f32[2,512,128]{1,2,0:T(8,128)S(1)} %fusion.71, bf16[2048,2,128]{0,2,1:T(8,128)(2,1)S(1)} %copy-done.2, f32[2,512,2048]{2,1,0:T(8,128)S(1)} %get-tuple-element.210, f32[2,512]{1,0:T(2,128)S(1)} %max.9, pred[2048]{0:T(1024)(128)(4,1)S(1)} %broadcast_in_dim.164, ...), kind=kOutput, calls=%fused_computation.19.clone.1 | convolution fusion | flops 545652736 | bytes 10233856 | tf_op jit(solution)/shard_map/while/body/eval_jaxpr/hqk,khd->qhd/dot_general | solution.py:82
  182.1 20.7 %all_to_all.39 = bf16[8,128,256]{2,1,0:T(8,128)(2,1)S(1)} all-to-all(bf16[8,128,256]{2,1,0:T(8,128)(2,1)S(1)} %bitcast.88), channel_id=1, replica_groups=mesh['x'=4,'z'=8,'y_lo'=2,'y_hi'=4,'core'=2] {'y_hi','core'}, dimensions={0} | all-to-all | bytes 1048576 | tf_op jit(solution)/shard_map/all_to_all | solution.py:99
  203.1 5.5 %fusion.39 = bf16[1,128,2048]{2,1,0:T(8,128)(2,1)} fusion(bf16[128,2048]{0,1:T(8,128)(2,1)S(1)} %bitcast.85, bf16[2048,2048]{1,0:T(8,128)(2,1)} %all-gather.6.cloned.1.call-done), kind=kOutput, calls=%fused_computation.38 | convolution fusion | flops 1074003968 | bytes 9437184 | tf_op jit(solution)/shard_map/dot_general | solution.py:100
  (70 shorter events, 25.2 us)
Async XLA Ops:
  6.5 69.5 %all-gather.4.cloned.1.call-start = ((), (), s32[]{:S(2)}) async-start(), calls=%async_computation.3 | async-start | bytes 2359296 | tf_op jit(solution)/shard_map/all_gather | solution.py:29
  33.2 7.9 %copy-start.5 = (s32[128]{0:T(128)S(1)}, s32[128]{0:T(128)}, u32[]{:S(2)}) copy-start(s32[128]{0:T(128)} %param.9) | copy-start | bytes 1540
  33.2 8.1 %copy-start.6 = (s32[64]{0:T(128)S(1)}, s32[64]{0:T(128)}, u32[]{:S(2)}) copy-start(s32[64]{0:T(128)} %param.10) | copy-start | bytes 772
  33.2 45.3 %all-to-all-start.1 = ((bf16[128,8,768]{0,2,1:T(8,128)(2,1)}), bf16[128,8,768]{0,2,1:T(8,128)(2,1)}, u32[]{:S(2)}, u32[]{:S(2)}) async-start(bf16[128,8,768]{0,2,1:T(8,128)(2,1)} %bitcast.1), calls=%async_computation.1 | async-start | bytes 3145728 | tf_op jit(solution)/shard_map/all_to_all | solution.py:31
  78.6 63.1 %all-to-all-start = ((bf16[64,2,16,512]{3,2,1,0:T(8,128)(2,1)}), bf16[64,2,16,512]{3,2,1,0:T(8,128)(2,1)S(1)}, u32[]{:S(2)}, u32[]{:S(2)}) async-start(bf16[64,2,16,512]{3,2,1,0:T(8,128)(2,1)} %bitcast.83), calls=%async_computation | async-start | bytes 4194304 | tf_op jit(solution)/shard_map/all_to_all | solution.py:50
  92.1 111.0 %all-gather.6.cloned.1.call-start = ((), (), s32[]{:S(2)}) async-start(), calls=%async_computation.4 | async-start | bytes 10485760 | tf_op jit(solution)/shard_map/all_gather | solution.py:49
  141.7 2.6 %copy-start.1 = (bf16[64,2,16,512]{3,2,1,0:T(8,128)(2,1)}, bf16[64,2,16,512]{3,2,1,0:T(8,128)(2,1)S(1)}, u32[]{:S(2)}) copy-start(bf16[64,2,16,512]{3,2,1,0:T(8,128)(2,1)S(1)} %all-to-all-done) | copy-start | bytes 6291460
  150.9 3.8 %copy-start.3 = (bf16[2,512,256]{2,1,0:T(8,128)(2,1)S(1)}, bf16[2,512,256]{2,1,0:T(8,128)(2,1)}, u32[]{:S(2)}) copy-start(bf16[2,512,256]{2,1,0:T(8,128)(2,1)} %custom-call) | copy-start | bytes 1572868
  159.3 2.3 %copy-start = (f32[2,512,1024]{2,1,0:T(8,128)S(1)}, f32[2,512,1024]{2,1,0:T(8,128)}, u32[]{:S(2)}) copy-start(f32[2,512,1024]{2,1,0:T(8,128)} %get-tuple-element.207) | copy-start | bytes 12582916 | tf_op jit(solution)/shard_map/while
  162.8 1.9 copy-start.4
  164.7 1.4 copy-start.2
  173.1 2.2 %copy-start = (f32[2,512,1024]{2,1,0:T(8,128)S(1)}, f32[2,512,1024]{2,1,0:T(8,128)}, u32[]{:S(2)}) copy-start(f32[2,512,1024]{2,1,0:T(8,128)} %get-tuple-element.207) | copy-start | bytes 12582916 | tf_op jit(solution)/shard_map/while
  176.5 1.9 copy-start.4
  178.3 1.4 copy-start.2
Sparse Core Ops, SparseCore 0:
  30.7 45.2 all-gather.3
  95.0 97.7 all-gather.5
where the time goes:
time: 216 us; the launch traced here: 215 us
  waiting for transfers between devices  72 us (33%)
  blocking collectives  44.8 us (21%)
  local copies, waits for them, and re-layouts  32.8 us (15%)
  matrix products  21.8 us (10%)
  starting transfers between devices  18.4 us (9%)
  between operations  13.5 us (6%)
  other arithmetic  11.8 us (5%)
    all_to_all x1, waiting for transfers between devices, per_device(): lax.all_to_all(packed, DP, split_axis=0, concat_axis=0, tiled=True)  37.4 us
    all_gather x1, waiting for transfers between devices, per_device(): weight = lax.all_gather(weight, DP[1], axis=0, tiled=True)  31.3 us
    all_gather x3, blocking collectives, per_device(): weight = lax.all_gather(weight, name, axis=0, tiled=True)  24 us
    all_to_all x1, blocking collectives, per_device(): lax.all_to_all(attn_heads, FSDP, split_axis=0, concat_axis=1, tiled=True)  20.7 us
    all_to_all x1, starting transfers between devices, per_device(): lax.all_to_all(packed, DP, split_axis=0, concat_axis=0, tiled=True)  13.5 us
    unnamed x12, local copies, waits for them, and re-layouts  6.55 us
    reduce_sum x4, other arithmetic, attend(): row_total = jnp.sum(cache_expo, axis=2) + jnp.sum(group_expo, axis=2)  6.12 us
    dot_general x2, matrix products, attend(): jnp.einsum('qhd,khd->hqk', query_block, new_keys, preferred_element_type=...  5.78 us
  transfers between devices with their start and end apart: 4, of which 3 were waited for; matrix products, arithmetic and copies ran while one was open for 28% of the time, Pallas kernels for 0%

commit v1 on v0

--- a/solution.py
+++ b/solution.py
@@ -26,7 +26,9 @@
     for name in reversed(DP[2:] + FSDP):
         weight = lax.all_gather(weight, name, axis=0, tiled=True)
     weight, group_qkv = lax.optimization_barrier((weight, group_qkv))
-    weight = lax.all_gather(weight, DP[1], axis=0, tiled=True)
+    weight = jnp.concatenate(
+        lax.all_to_all(jnp.stack([weight] * lax.axis_size(DP[1])), DP[1], 0, 0), axis=0
+    )
     local_qkv = group_qkv.reshape(tokens_here, fsdp_count, heads_here * 3 * HD)
     gathered_qkv = lax.all_to_all(local_qkv, FSDP, split_axis=1, concat_axis=0, tiled=True)
     group_len = tokens_here * fsdp_count

time: 216 us -> 264 us (1.22)
  the two profiles are of different devices: /device:TPU:64 before, /device:TPU:1 now
where the time goes in v1:
time: 264 us; the launch traced here: 263 us
  waiting for transfers between devices  112 us (42%)
  blocking collectives  48.3 us (18%)
  local copies, waits for them, and re-layouts  34.4 us (13%)
  matrix products  21.8 us (8%)
  starting transfers between devices  21.2 us (8%)
  between operations  13.5 us (5%)
  other arithmetic  11.8 us (4%)
    all_to_all x1, waiting for transfers between devices, per_device(): lax.all_to_all(jnp.stack([weight] * lax.axis_size(DP[1])), DP[1], 0, 0)  45.2 us
    all_to_all x1, waiting for transfers between devices, per_device(): lax.all_to_all(packed, DP, split_axis=0, concat_axis=0, tiled=True)  35.3 us
    all_to_all x1, waiting for transfers between devices, per_device(): lax.all_to_all(local_qkv, FSDP, split_axis=1, concat_axis=0, tiled=True)  30.6 us
    all_to_all x1, blocking collectives, per_device(): lax.all_to_all(attn_heads, FSDP, split_axis=0, concat_axis=1, tiled=True)  24.4 us
    all_gather x3, blocking collectives, per_device(): weight = lax.all_gather(weight, name, axis=0, tiled=True)  23.9 us
    all_to_all x1, starting transfers between devices, per_device(): lax.all_to_all(local_qkv, FSDP, split_axis=1, concat_axis=0, tiled=True)  8.88 us
    all_to_all x1, starting transfers between devices, per_device(): lax.all_to_all(jnp.stack([weight] * lax.axis_size(DP[1])), DP[1], 0, 0)  7.28 us
    unnamed x14, local copies, waits for them, and re-layouts  6.56 us
  transfers between devices with their start and end apart: 4, of which 3 were waited for; matrix products, arithmetic and copies ran while one was open for 23% of the time, Pallas kernels for 0%

profile of v1, /device:TPU:1, one launch (start us, length us, event | category | flops | bytes accessed | tf_op | source)
XLA Modules:
  0.0 263.1 jit_solution(13853678462268318374)
XLA Ops:
  6.5 8.5 %all-gather = bf16[2,4,2048]{2,1,0:T(4,128)(2,1)S(1)} all-gather(bf16[1,4,2048]{2,1,0:T(4,128)(2,1)} %bitcast.92), channel_id=1, replica_groups=mesh['x'=4,'z'=8,'y_lo'=2,'y_hi'=4,'core'=2] {'core'}, dimensions={0}, use_global_device_ids=true | all-gather | bytes 49152 | tf_op jit(solution)/shard_map/all_gather | solution.py:27
  15.1 10.9 %all_gather.13 = bf16[32,2048]{1,0:T(8,128)(2,1)S(1)} all-gather(bf16[8,2048]{1,0:T(8,128)(2,1)S(1)} %reshape.90), channel_id=1, replica_groups=mesh['x'=4,'z'=8,'y_lo'=2,'y_hi'=4,'core'=2] {'y_hi'}, dimensions={0}, use_global_device_ids=true | all-gather | bytes 163840 | tf_op jit(solution)/shard_map/all_gather | solution.py:27
  26.0 4.5 %all_gather.14 = bf16[64,2048]{1,0:T(8,128)(2,1)S(1)} all-gather(bf16[32,2048]{1,0:T(8,128)(2,1)S(1)} %all_gather.13), channel_id=1, replica_groups=mesh['x'=4,'z'=8,'y_lo'=2,'y_hi'=4,'core'=2] {'y_lo'}, dimensions={0}, use_global_device_ids=true | all-gather | bytes 393216 | tf_op jit(solution)/shard_map/all_gather | solution.py:27
  32.1 7.3 %all-to-all-start = ((bf16[8,64,2048]{2,1,0:T(8,128)(2,1)}), bf16[8,64,2048]{2,1,0:T(8,128)(2,1)S(1)}, u32[]{:S(2)}, u32[]{:S(2)}) async-start(bf16[8,64,2048]{2,1,0:T(8,128)(2,1)} %stack.2), calls=%async_computation | async-start | bytes 4194304 | tf_op jit(solution)/shard_map/all_to_all | solution.py:30
  39.3 2.6 copy.38
  41.9 45.2 %all-to-all-done = bf16[8,64,2048]{2,1,0:T(8,128)(2,1)S(1)} async-done(((bf16[8,64,2048]{2,1,0:T(8,128)(2,1)}), bf16[8,64,2048]{2,1,0:T(8,128)(2,1)S(1)}, u32[]{:S(2)}, u32[]{:S(2)}) %all-to-all-start) | async-done | bytes 2097184 | tf_op jit(solution)/shard_map/all_to_all | solution.py:30
  87.1 8.9 %all-to-all-start.2 = ((bf16[128,8,768]{0,2,1:T(8,128)(2,1)}), bf16[128,8,768]{0,2,1:T(8,128)(2,1)}, u32[]{:S(2)}, u32[]{:S(2)}) async-start(bf16[128,8,768]{0,2,1:T(8,128)(2,1)} %bitcast.87), calls=%async_computation.2 | async-start | bytes 3145728 | tf_op jit(solution)/shard_map/all_to_all | solution.py:33
  96.0 3.0 %copy.51 = bf16[16,8,16,512]{3,1,2,0:T(8,128)(2,1)S(1)} copy(bf16[16,8,16,512]{3,2,1,0:T(8,128)(2,1)} %bitcast.89) | data formatting | bytes 4194304
  100.4 2.2 copy.52
  102.7 30.6 %all-to-all-done.2 = bf16[128,8,768]{0,2,1:T(8,128)(2,1)} async-done(((bf16[128,8,768]{0,2,1:T(8,128)(2,1)}), bf16[128,8,768]{0,2,1:T(8,128)(2,1)}, u32[]{:S(2)}, u32[]{:S(2)}) %all-to-all-start.2) | async-done | bytes 1572896 | tf_op jit(solution)/shard_map/all_to_all | solution.py:33
  133.3 5.0 %all-to-all-start.1 = ((bf16[64,2,16,512]{3,2,1,0:T(8,128)(2,1)}), bf16[64,2,16,512]{3,2,1,0:T(8,128)(2,1)S(1)}, u32[]{:S(2)}, u32[]{:S(2)}) async-start(bf16[64,2,16,512]{3,2,1,0:T(8,128)(2,1)} %bitcast.85), calls=%async_computation.1 | async-start | bytes 4194304 | tf_op jit(solution)/shard_map/all_to_all | solution.py:52
  139.1 3.6 %copy.39 = bf16[8,128,1,768]{1,0,3,2:T(8,128)(2,1)} copy(bf16[8,128,1,768]{1,3,0,2:T(8,128)(2,1)} %bitcast.3) | data formatting | bytes 3145728 | tf_op jit(solution)/shard_map/all_to_all | solution.py:33
  142.7 3.7 %reshape.86 = bf16[1024,2,3,128]{0,3,2,1:T(8,128)(2,1)} reshape(bf16[8,128,1,768]{1,0,3,2:T(8,128)(2,1)} %copy.39) | data formatting | bytes 3145728 | tf_op jit(solution)/shard_map/reshape | solution.py:35
  146.4 2.5 slice_bitcast_fusion
  150.5 35.3 %all-to-all-done.1 = bf16[64,2,16,512]{3,2,1,0:T(8,128)(2,1)S(1)} async-done(((bf16[64,2,16,512]{3,2,1,0:T(8,128)(2,1)}), bf16[64,2,16,512]{3,2,1,0:T(8,128)(2,1)S(1)}, u32[]{:S(2)}, u32[]{:S(2)}) %all-to-all-start.1) | async-done | bytes 2097184 | tf_op jit(solution)/shard_map/all_to_all | solution.py:52
  185.7 2.4 not_reduce_fusion
  188.5 2.6 reshape.87
  191.0 3.9 %fusion.43 = (bf16[2048,2,1,128]{3,2,1,0:T(2,128)(2,1)S(1)}, bf16[2048,2,1,128]{3,2,1,0:T(2,128)(2,1)}) fusion(bf16[2048,2,2,128]{3,2,1,0:T(2,128)(2,1)S(1)} %reshape.87), kind=kLoop, calls=%fused_computation.54 | loop fusion | bytes 4194304 | tf_op jit(solution)/shard_map/slice | solution.py:58
  198.7 27.4 %while.11 = (s32[]{:T(128)}, bf16[2,512,256]{2,1,0:T(8,128)(2,1)S(1)}, bf16[2,512,2,128]{3,1,0,2:T(8,128)(2,1)S(1)}, bf16[2048,2,128]{2,0,1:T(8,128)(2,1)S(1)}, ...) while((s32[]{:T(128)}, ...), condition=%wide.region_10.11_spmd.clone, body=%wide.region_5.10_spmd.clone.sunk | while | flops 1646131712 | bytes 69022040 | solution.py:100
  200.3 2.9 %fusion.69 = (f32[2,512]{1,0:T(2,128)S(1)}, f32[2,512,1024]{2,1,0:T(8,128)}) fusion(pred[512,1024]{1,0:T(8,128)(4,1)S(1)} %iota_compare_fusion.5, bf16[1024,2,128]{2,0,1:T(8,128)(2,1)S(1)} %get-tuple-element.236, bf16[2,512,2,128]{3,1,0,2:T(8,128)(2,1)S(1)} %get-tuple-element.233, s32[]{:T(128)} %get-tuple-element.221), kind=kOutput, calls=%fused_computation.10.clone.1 | convolution fusion | flops 271580160 | bytes 5509124 | tf_op jit(solution)/shard_map/while/body/eval_jaxpr/qhd,khd->hqk/dot_general | solution.py:75
  214.1 2.9 %fusion.69 = (f32[2,512]{1,0:T(2,128)S(1)}, f32[2,512,1024]{2,1,0:T(8,128)}) fusion(pred[512,1024]{1,0:T(8,128)(4,1)S(1)} %iota_compare_fusion.5, bf16[1024,2,128]{2,0,1:T(8,128)(2,1)S(1)} %get-tuple-element.236, bf16[2,512,2,128]{3,1,0,2:T(8,128)(2,1)S(1)} %get-tuple-element.233, s32[]{:T(128)} %get-tuple-element.221), kind=kOutput, calls=%fused_computation.10.clone.1 | convolution fusion | flops 271580160 | bytes 5509124 | tf_op jit(solution)/shard_map/while/body/eval_jaxpr/qhd,khd->hqk/dot_general | solution.py:75
  223.8 2.2 fusion.74
  226.1 24.4 %all_to_all.44 = bf16[8,128,256]{2,1,0:T(8,128)(2,1)S(1)} all-to-all(bf16[8,128,256]{2,1,0:T(8,128)(2,1)S(1)} %bitcast.91), channel_id=1, replica_groups=mesh['x'=4,'z'=8,'y_lo'=2,'y_hi'=4,'core'=2] {'y_hi','core'}, dimensions={0} | all-to-all | bytes 1048576 | tf_op jit(solution)/shard_map/all_to_all | solution.py:101
  250.8 5.5 %fusion.39 = bf16[1,128,2048]{2,1,0:T(8,128)(2,1)} fusion(bf16[128,2048]{0,1:T(8,128)(2,1)S(1)} %bitcast.88, bf16[2048,2048]{1,0:T(8,128)(2,1)} %all-gather.3.cloned.1.call-done), kind=kOutput, calls=%fused_computation.38 | convolution fusion | flops 1074003968 | bytes 9437184 | tf_op jit(solution)/shard_map/dot_general | solution.py:102
  (72 shorter events, 29.0 us)
Async XLA Ops:
  32.1 55.1 %all-to-all-start = ((bf16[8,64,2048]{2,1,0:T(8,128)(2,1)}), bf16[8,64,2048]{2,1,0:T(8,128)(2,1)S(1)}, u32[]{:S(2)}, u32[]{:S(2)}) async-start(bf16[8,64,2048]{2,1,0:T(8,128)(2,1)} %stack.2), calls=%async_computation | async-start | bytes 4194304 | tf_op jit(solution)/shard_map/all_to_all | solution.py:30
  41.9 57.1 %copy-start.6 = (s32[128]{0:T(128)S(1)}, s32[128]{0:T(128)}, u32[]{:S(2)}) copy-start(s32[128]{0:T(128)} %param.9) | copy-start | bytes 1540
  41.9 57.4 %copy-start.7 = (s32[64]{0:T(128)S(1)}, s32[64]{0:T(128)}, u32[]{:S(2)}) copy-start(s32[64]{0:T(128)} %param.10) | copy-start | bytes 772
  87.1 8.9 %copy-start.2 = (bf16[8,64,2048]{2,1,0:T(8,128)(2,1)}, bf16[8,64,2048]{2,1,0:T(8,128)(2,1)S(1)}, u32[]{:S(2)}) copy-start(bf16[8,64,2048]{2,1,0:T(8,128)(2,1)S(1)} %all-to-all-done) | copy-start | bytes 6291460
  87.1 46.1 %all-to-all-start.2 = ((bf16[128,8,768]{0,2,1:T(8,128)(2,1)}), bf16[128,8,768]{0,2,1:T(8,128)(2,1)}, u32[]{:S(2)}, u32[]{:S(2)}) async-start(bf16[128,8,768]{0,2,1:T(8,128)(2,1)} %bitcast.87), calls=%async_computation.2 | async-start | bytes 3145728 | tf_op jit(solution)/shard_map/all_to_all | solution.py:33
  133.3 52.5 %all-to-all-start.1 = ((bf16[64,2,16,512]{3,2,1,0:T(8,128)(2,1)}), bf16[64,2,16,512]{3,2,1,0:T(8,128)(2,1)S(1)}, u32[]{:S(2)}, u32[]{:S(2)}) async-start(bf16[64,2,16,512]{3,2,1,0:T(8,128)(2,1)} %bitcast.85), calls=%async_computation.1 | async-start | bytes 4194304 | tf_op jit(solution)/shard_map/all_to_all | solution.py:52
  138.3 112.5 %all-gather.3.cloned.1.call-start = ((), (), s32[]{:S(2)}) async-start(), calls=%async_computation.4 | async-start | bytes 10485760 | tf_op jit(solution)/shard_map/all_gather | solution.py:51
  185.7 2.6 copy-start.1
  194.9 3.8 %copy-start.4 = (bf16[2,512,256]{2,1,0:T(8,128)(2,1)S(1)}, bf16[2,512,256]{2,1,0:T(8,128)(2,1)}, u32[]{:S(2)}) copy-start(bf16[2,512,256]{2,1,0:T(8,128)(2,1)} %custom-call) | copy-start | bytes 1572868
  203.4 2.3 copy-start
  206.9 1.9 copy-start.5
  208.7 1.4 copy-start.3
  217.1 2.2 copy-start
  220.5 1.9 copy-start.5
  222.4 1.4 copy-start.3
Sparse Core Ops, SparseCore 0:
  141.2 100.7 all-gather.2
